TPU v7x, 32 devices: a whole 2x2x4 slice. The times are simulated.
32 devices in a mesh: col: 8 (over y, x, core), row: 4 (over z).
Axes of the slice: x: 2, y: 2, z: 4, core: 2. Of those that a mesh axis runs over, the one named last changes fastest.
Arguments:
- p_blocks: bfloat16 [4, 72, 4096], P('row', 'col'), may hold values from -0.5390625 to 0.5390625
- p_slots: int32 [4, 72], P('row', 'col'), may hold values from 0 to 18, as said below
- out_slots: int32 [4, 104], P('row', 'col'), may hold values from 0 to 18, as said below
Outputs:
- purified: float32 [4, 104, 4096], P('row', 'col')
Inputs may be any that keep to these rules, and one draw needn't show every extreme that they name: `p_slots`: on each device the used slots (entries below 18) come first and name distinct positions; the remaining slots hold 18. Each device uses between half of its 9 slots (rounded up) and all of them, and some device uses all. `out_slots`: on each device the used slots (entries below 18) come first and name distinct positions; the remaining slots hold 18. Each device uses between half of its 13 slots (rounded up) and all of them, and some device uses all.
All inputs are finite; a program needn't handle non-finite values.
Results may differ from a plain program's by a relative error of at most 0.0003.
Values may be sent and summed in bfloat16 or wider, within the bound.
No kernel may reach another device: no remote copies, remote signals or barrier semaphores. Data moves between devices by JAX's collectives and lax.ppermute only.
A program may use at most 192 MiB of HBM per device.

v0:
```python
from functools import partial
import jax
import jax.numpy as jnp
from jax import lax
from jax.sharding import PartitionSpec as P

BLK = 64
COLS_DEV = 3


def add_terms(accum, portion, offset, table, capacity, rows_dev, block_edge, full_precision):
    block_vals, slot_ids = portion
    amount = slot_ids.shape[0]
    source = jnp.arange(amount, dtype=jnp.int32) // capacity
    local_row = slot_ids // COLS_DEV
    panel_row = source * COLS_DEV + slot_ids % COLS_DEV
    matching = table[panel_row]
    left = block_vals.reshape(amount, block_edge, block_edge)
    products = jnp.einsum("mab,mbw->maw", left, matching, preferred_element_type=jnp.float32)
    selector = (local_row[:, None] == jnp.arange(rows_dev, dtype=jnp.int32)[None, :]).astype(
        jnp.float32
    )
    return accum + jnp.einsum(
        "mr,maw->raw",
        selector,
        products,
        precision=lax.Precision.HIGHEST,
        preferred_element_type=jnp.float32,
    )


def on_device(p_blocks, p_slots, out_slots):
    n_row = lax.axis_size("row")
    n_col = lax.axis_size("col")
    capacity = p_slots.shape[1]
    block_edge = BLK
    rows_dev = COLS_DEV * n_col // n_row
    cells = rows_dev * COLS_DEV
    blocks_total = rows_dev * n_row
    width = COLS_DEV * block_edge
    own_blocks = p_blocks[0]
    own_ids = p_slots[0]
    down_blocks, down_ids = (
        lax.all_gather(own_blocks, "row", axis=0, tiled=True),
        lax.all_gather(own_ids, "row", axis=0, tiled=True),
    )
    source = jnp.arange(n_row * capacity, dtype=jnp.int32) // capacity
    panel_row = source * rows_dev + down_ids // COLS_DEV
    flat_index = jnp.where(
        down_ids < cells, panel_row * COLS_DEV + down_ids % COLS_DEV, blocks_total * COLS_DEV
    )
    column_panel = jnp.zeros((blocks_total * COLS_DEV, block_edge * block_edge), jnp.bfloat16)
    column_panel = column_panel.at[flat_index].set(down_blocks, mode="drop")
    column_panel = column_panel.reshape(blocks_total, COLS_DEV, block_edge, block_edge)
    column_panel = column_panel.transpose(0, 2, 1, 3).reshape(blocks_total, block_edge, width)
    empty = jnp.zeros((rows_dev, block_edge, width), jnp.float32)
    first_terms = partial(
        add_terms,
        table=column_panel,
        capacity=capacity,
        rows_dev=rows_dev,
        block_edge=block_edge,
        full_precision=False,
    )
    square = first_terms(
        empty,
        (
            lax.all_gather(own_blocks, "col", axis=0, tiled=True),
            lax.all_gather(own_ids, "col", axis=0, tiled=True),
        ),
        jnp.int32(0),
    )
    square_flat = square.reshape(rows_dev * block_edge, width)
    column_matrix = column_panel.reshape(blocks_total * block_edge, width).astype(jnp.float32)
    cube = jnp.dot(
        lax.all_gather(square_flat, "col", axis=1, tiled=True),
        column_matrix,
        precision=lax.Precision.HIGHEST,
        preferred_element_type=jnp.float32,
    )
    combined = 3.0 * square_flat - 2.0 * cube
    new_grid = combined.reshape(rows_dev, block_edge, COLS_DEV, block_edge).transpose(0, 2, 1, 3)
    new_grid = new_grid.reshape(cells, block_edge * block_edge)
    out_ids = out_slots[0]
    picked = new_grid[jnp.minimum(out_ids, cells - 1)]
    picked = jnp.where((out_ids < cells)[:, None], picked, jnp.zeros_like(picked))
    return picked[None]


def solution(mesh):
    in_specs = (P("row", "col", None), P("row", "col"), P("row", "col"))
    out_specs = P("row", "col", None)
    return jax.shard_map(
        on_device, mesh=mesh, in_specs=in_specs, out_specs=out_specs, check_vma=False
    )
```

profile of v0, /device:TPU:0, one launch (start us, length us, event | category | flops | bytes accessed | tf_op | source)
XLA Modules:
  0.0 116.2 jit_solution(5685451700651422301)
XLA Ops:
  6.5 0.0 copy-start.4
  6.5 0.0 copy-start.3
  6.5 0.0 copy-start.1
  6.5 0.0 all-gather.6.cloned.1.call-start
  6.5 1.1 copy.30
  7.6 18.3 %all-gather.2 = bf16[1,36,4096]{2,0,1:T(2,128)(2,1)S(1)} all-gather(bf16[1,9,4096]{2,0,1:T(2,128)(2,1)S(1)} %copy.30), channel_id=4, replica_groups=mesh['col'=8,'row'=4] {'row'}, dimensions={1}, use_global_device_ids=true | all-gather | bytes 368640 | tf_op jit(solution)/shard_map/all_gather | solution.py:44
  25.9 11.5 %all-gather.3 = bf16[1,72,4096]{2,0,1:T(2,128)(2,1)S(1)} all-gather(bf16[1,9,4096]{2,0,1:T(2,128)(2,1)S(1)} %copy.30), channel_id=5, replica_groups=mesh['col'=8,'row'=4] {'col'}, dimensions={1}, use_global_device_ids=true | all-gather | bytes 663552 | tf_op jit(solution)/shard_map/all_gather | solution.py:68
  37.4 0.0 copy-done.4
  37.4 0.7 dynamic-slice.1
  38.1 0.0 copy-done.3
  38.1 0.6 dynamic-slice
  40.0 0.0 copy-done.1
  40.0 0.1 bitcast_dynamic-update-slice_fusion.1
  40.1 7.0 %all-reduce = s32[72]{0:T(128)S(1)} all-reduce(s32[72]{0:T(128)S(1)} %get-tuple-element.7), channel_id=2, replica_groups=mesh['col'=8,'row'=4] {'col'}, use_global_device_ids=true, to_apply=%add | all-reduce | flops 72 | bytes 576
  47.2 8.0 %all-reduce.1 = s32[36]{0:T(128)S(1)} all-reduce(s32[36]{0:T(128)S(1)} %get-tuple-element.8), channel_id=3, replica_groups=mesh['col'=8,'row'=4] {'row'}, use_global_device_ids=true, to_apply=%add.1 | all-reduce | flops 36 | bytes 288
  55.2 1.5 %scatter_custom_fusion = bf16[72,4096]{1,0:T(8,128)(2,1)S(1)} fusion(s32[36]{0:T(128)S(1)} %compare_select_fusion.2, bf16[1,36,4096]{2,0,1:T(2,128)(2,1)S(1)} %all-gather.2, bf16[]{:T(256)} %constant.56.clone.1), kind=kCustom, calls=%fused_computation.8 | custom fusion | bytes 1179650 | tf_op jit(solution)/shard_map/scatter | solution.py:53
  56.7 1.3 %reshape.73 = bf16[24,3,64,64]{3,2,1,0:T(8,128)(2,1)S(1)} reshape(bf16[72,4096]{1,0:T(8,128)(2,1)S(1)} %scatter_custom_fusion) | data formatting | bytes 1179648 | tf_op jit(solution)/shard_map/reshape | solution.py:54
  58.0 3.6 %reduce = bf16[72,4096]{1,0:T(8,128)(2,1)S(1)} reduce(bf16[1,72,4096]{2,0,1:T(2,128)(2,1)S(1)} %all-gather.3, bf16[]{:T(256)} %constant.80), dimensions={0}, to_apply=%all-gather.3.reduce_sub_computation | reduce | bytes 1179650 | tf_op jit(solution)/shard_map/all_gather | solution.py:68
  61.5 1.3 %reshape.75 = bf16[72,64,64]{2,1,0:T(8,128)(2,1)S(1)} reshape(bf16[72,4096]{1,0:T(8,128)(2,1)S(1)} %reduce) | data formatting | bytes 1179648 | tf_op jit(solution)/shard_map/reshape | solution.py:18
  62.8 0.9 copy.31
  63.7 3.0 %gather_fusion = bf16[72,64,192]{1,2,0:T(8,128)(2,1)} fusion(bf16[24,64,192]{1,2,0:T(8,128)(2,1)S(1)} %bitcast.40, s32[1024]{0:T(1024)S(1)} %pad_clamp_fusion.1), kind=kCustom, calls=%fused_computation | custom fusion | bytes 3539232 | tf_op jit(solution)/shard_map/gather | solution.py:17
  66.7 4.4 %convolution_bitcast_fusion = f32[72,64,192]{2,1,0:T(8,128)S(1)} fusion(bf16[72,64,192]{1,2,0:T(8,128)(2,1)} %gather_fusion, bf16[72,64,64]{2,1,0:T(8,128)(2,1)S(1)} %reshape.75), kind=kOutput, calls=%fused_computation.5 | convolution fusion | flops 113246208 | bytes 5898240 | tf_op jit(solution)/shard_map/mab,mbw->maw/dot_general | solution.py:19
  71.1 4.3 %fusion = f32[6,64,192]{2,0,1:T(8,128)S(1)} fusion(f32[72,64,192]{2,1,0:T(8,128)S(1)} %convolution_bitcast_fusion, s32[72]{0:T(128)S(1)} %get-tuple-element.5), kind=kOutput, calls=%fused_computation.3 | convolution fusion | flops 63701424 | bytes 3834144 | tf_op jit(solution)/shard_map/mr,maw->raw/dot_general | solution.py:23
  75.4 0.1 copy.35
  75.5 0.9 copy.36
  76.4 0.0 copy-start.2
  76.4 0.0 copy-start
  76.4 0.0 all-gather.6.cloned.1.call-update
  76.4 1.3 %copy.38 = bf16[24,64,3,64]{1,0,3,2:T(8,128)(2,1)S(1)} copy(bf16[24,64,3,64]{3,1,2,0:T(8,128)(2,1)S(1)} %bitcast.39) | data formatting | bytes 1179648 | tf_op jit(solution)/shard_map/transpose | solution.py:55
  77.8 0.7 reshape_reshape.3
  78.5 0.0 copy-done.2
  78.5 25.6 %all-gather.6.cloned.1.call-done = f32[384,1536]{0,1:T(8,128)} async-done(((f32[384,192]{0,1:T(8,128)}), f32[384,1536]{0,1:T(8,128)}) %all-gather.6.cloned.1.call-update) | async-done | bytes 2359312 | tf_op jit(solution)/shard_map/all_gather | solution.py:76
  104.1 0.0 copy-done
  104.1 2.9 %fusion.2 = f32[384,192]{0,1:T(8,128)S(1)} fusion(f32[384,1536]{0,1:T(8,128)} %all-gather.6.cloned.1.call-done, bf16[1536,192]{0,1:T(8,128)(2,1)S(1)} %reshape_reshape.3, f32[384,192]{0,1:T(8,128)S(1)} %copy-done), kind=kOutput, calls=%fused_computation.7 | convolution fusion | flops 1359175680 | bytes 3538944 | tf_op jit(solution)/shard_map/dot_general | solution.py:75
  107.1 0.2 reshape.77
  107.3 0.3 copy.39
  107.5 0.2 reshape.78
  107.7 0.6 gather_fusion.1
  108.4 0.1 bitcast_select_fusion
  108.5 0.9 copy.40
  (8 shorter events, 0.1 us)
Async XLA Ops:
  6.5 30.9 %copy-start.4 = (u32[32]{0:T(128)S(1)}, u32[32]{0:T(128)}, u32[]{:S(2)}) copy-start(u32[32]{0:T(128)} %constant.75) | copy-start | bytes 388
  6.5 31.5 %copy-start.3 = (u32[32]{0:T(128)S(1)}, u32[32]{0:T(128)}, u32[]{:S(2)}) copy-start(u32[32]{0:T(128)} %constant.70) | copy-start | bytes 388
  6.5 33.5 %copy-start.1 = (s32[1,9]{1,0:T(1,128)S(1)}, s32[1,9]{1,0:T(1,128)}, u32[]{:S(2)}) copy-start(s32[1,9]{1,0:T(1,128)} %param.4) | copy-start | bytes 112
  6.5 97.6 %all-gather.6.cloned.1.call-start = ((), (), s32[]{:S(2)}) async-start(), calls=%async_computation | async-start | bytes 2654208 | tf_op jit(solution)/shard_map/all_gather | solution.py:76
  76.4 2.1 %copy-start.2 = (s32[1,13]{1,0:T(1,128)S(1)}, s32[1,13]{1,0:T(1,128)}, u32[]{:S(2)}) copy-start(s32[1,13]{1,0:T(1,128)} %param.5) | copy-start | bytes 160
  76.4 27.7 %copy-start = (f32[384,192]{0,1:T(8,128)S(1)}, f32[384,192]{0,1:T(8,128)}, u32[]{:S(2)}) copy-start(f32[384,192]{0,1:T(8,128)} %copy.36) | copy-start | bytes 884740
Sparse Core Ops, SparseCore 0:
  76.5 27.5 all-gather.5
where the time goes:
time: 116 us
  blocking collectives  44.8 us (39%)
  waiting for transfers between devices  25.6 us (22%)
  local copies, waits for them, and re-layouts  15.6 us (13%)
  between operations  14.9 us (13%)
  matrix products  11.6 us (10%)
  other arithmetic  3.71 us (3%)
    all_gather x1, waiting for transfers between devices, on_device(): lax.all_gather(square_flat, 'col', axis=1, tiled=True)  25.6 us
    all_gather x1, blocking collectives, on_device(): lax.all_gather(own_blocks, 'row', axis=0, tiled=True)  18.3 us
    unnamed x2, blocking collectives  15 us
    all_gather x1, blocking collectives, on_device(): lax.all_gather(own_blocks, 'col', axis=0, tiled=True)  11.5 us
    dot_general x1, matrix products, add_terms(): jnp.einsum('mab,mbw->maw', left, matching, preferred_element_type=jnp.flo...  4.36 us
    dot_general x1, matrix products, add_terms(): jnp.einsum('mr,maw->raw', selector, products, precision=lax.Precision.HIG...  4.29 us
    all_gather x1, other arithmetic, on_device(): lax.all_gather(own_blocks, 'col', axis=0, tiled=True)  3.56 us
    gather x1, local copies, waits for them, and re-layouts, add_terms(): matching = table[panel_row]  3.03 us
  transfers between devices with their start and end apart: 1, of which 1 were waited for; matrix products, arithmetic and copies ran while one was open for 2% of the time, Pallas kernels for 0%

commit v1 on v0

--- a/solution.py
+++ b/solution.py
@@ -62,12 +62,33 @@
         block_edge=block_edge,
         full_precision=False,
     )
+
+    def spread_view(my_data, axis_id="col"):
+        piece_out = jax.lax.axis_size(axis_id)
+        mid_arr, all_rows, g_now = (piece_out, jax.lax.axis_index(axis_id), my_data.shape[0])
+        entries = tuple(((m, (m + 1) % mid_arr) for m in range(mid_arr)))
+        by_rank = tuple(((m, (m - 1) % mid_arr) for m in range(mid_arr)))
+        view_out = jnp.zeros(
+            (*my_data.shape[:0], mid_arr * g_now, *my_data.shape[1:]), my_data.dtype
+        )
+        view_out = lax.dynamic_update_slice_in_dim(view_out, my_data, all_rows * g_now, axis=0)
+        fresh = y2 = my_data
+        far_arr = mid_arr // 2
+        for ii in [*range(1, far_arr + 1)]:
+            fresh = jax.lax.ppermute(fresh, perm=entries, axis_name=axis_id)
+            view_out = lax.dynamic_update_slice_in_dim(
+                view_out, fresh, (all_rows - ii) % mid_arr * g_now, axis=0
+            )
+            if ii < mid_arr - far_arr:
+                y2 = jax.lax.ppermute(y2, axis_name=axis_id, perm=by_rank)
+                view_out = lax.dynamic_update_slice_in_dim(
+                    view_out, y2, (all_rows + ii) % mid_arr * g_now, axis=0
+                )
+        return view_out
+
     square = first_terms(
         empty,
-        (
-            lax.all_gather(own_blocks, "col", axis=0, tiled=True),
-            lax.all_gather(own_ids, "col", axis=0, tiled=True),
-        ),
+        (spread_view(own_blocks), lax.all_gather(own_ids, "col", axis=0, tiled=True)),
         jnp.int32(0),
     )
     square_flat = square.reshape(rows_dev * block_edge, width)

time: 116 us -> 123 us (1.060)
  local copies, waits for them, and re-layouts: 15.6 us -> 27.8 us
  blocking collectives: 44.8 us -> 32.8 us
  starting transfers between devices: 0.01 us -> 6.61 us
  other arithmetic: 3.71 us -> 0.15 us
  waiting for transfers between devices: 25.6 us -> 28.3 us
    all_gather x1 -> x0, blocking collectives: 11.5 us -> none  [on_device(): lax.all_gather(own_blocks, 'col', axis=0, tiled=True)]
    dynamic_update_slice x0 -> x8, local copies, waits for them, and re-layouts: none -> 10.5 us  [the longest x3 4.76 us: spread_view(): lax.dynamic_update_slice_in_dim(view_out, y2, (all_rows + ii) % mid_arr *...]
    ppermute x0 -> x7, starting transfers between devices: none -> 6.61 us  [the longest x3 6.11 us: spread_view(): y2 = jax.lax.ppermute(y2, axis_name=axis_id, perm=by_rank)]
    all_gather x1 -> x0, other arithmetic: 3.56 us -> none  [on_device(): lax.all_gather(own_blocks, 'col', axis=0, tiled=True)]
    all_gather x1, blocking collectives: 18.3 us -> 16.2 us  [on_device(): lax.all_gather(own_blocks, 'row', axis=0, tiled=True)]
    unnamed x16 -> x12, local copies, waits for them, and re-layouts: 2.44 us -> 4.27 us
    ppermute x0 -> x7, waiting for transfers between devices: none -> 1.82 us  [the longest x4 1.82 us: spread_view(): fresh = jax.lax.ppermute(fresh, perm=entries, axis_name=axis_id)]
    unnamed x2, blocking collectives: 15 us -> 16.6 us
  transfers between devices with their start and end apart: 1 -> 8, of which waited for: 1 -> 2; matrix products, arithmetic and copies ran while one was open for 2% -> 18% of each run, Pallas kernels for 0% -> 0%
where the time goes in v1:
time: 123 us; the launch traced here: 122 us
  blocking collectives  32.8 us (27%)
  waiting for transfers between devices  28.3 us (23%)
  local copies, waits for them, and re-layouts  27.8 us (23%)
  between operations  15 us (12%)
  matrix products  11.6 us (9%)
  starting transfers between devices  6.61 us (5%)
    all_gather x1, waiting for transfers between devices, on_device(): lax.all_gather(square_flat, 'col', axis=1, tiled=True)  26.5 us
    unnamed x2, blocking collectives  16.6 us
    all_gather x1, blocking collectives, on_device(): lax.all_gather(own_blocks, 'row', axis=0, tiled=True)  16.2 us
    ppermute x3, starting transfers between devices, spread_view(): y2 = jax.lax.ppermute(y2, axis_name=axis_id, perm=by_rank)  6.11 us
    dynamic_update_slice x3, local copies, waits for them, and re-layouts, spread_view(): lax.dynamic_update_slice_in_dim(view_out, y2, (all_rows + ii) % mid_arr *...  4.76 us
    dynamic_update_slice x4, local copies, waits for them, and re-layouts, spread_view(): lax.dynamic_update_slice_in_dim(view_out, fresh, (all_rows - ii) % mid_ar...  4.61 us
    dot_general x1, matrix products, add_terms(): jnp.einsum('mab,mbw->maw', left, matching, preferred_element_type=jnp.flo...  4.37 us
    dot_general x1, matrix products, add_terms(): jnp.einsum('mr,maw->raw', selector, products, precision=lax.Precision.HIG...  4.28 us
  transfers between devices with their start and end apart: 8, of which 2 were waited for; matrix products, arithmetic and copies ran while one was open for 18% of the time, Pallas kernels for 0%

profile of v1, /device:TPU:0, one launch (start us, length us, event | category | flops | bytes accessed | tf_op | source)
XLA Modules:
  0.0 122.2 jit_solution(5937367066940981621)
XLA Ops:
  6.5 3.4 %collective-permute-start.1 = (bf16[9,4096]{1,0:T(8,128)(2,1)}, bf16[9,4096]{1,0:T(8,128)(2,1)S(1)}, u32[]{:S(2)}, u32[]{:S(2)}) collective-permute-start(bf16[9,4096]{1,0:T(8,128)(2,1)} %bitcast.42), channel_id=1, source_target_pairs={{0,28},{4,0},{8,4},{12,8},{16,12},{20,16},{24,20},{28,24},{1,29},{... | collective-permute-start | bytes 221192 | tf_op jit(solution)/shard_map/ppermute | solution.py:83
  9.9 0.0 collective-permute-start
  9.9 1.2 %dynamic-slice.1 = u32[1]{0:T(128)} dynamic-slice(u32[32]{0:T(128)} %constant.129, u32[]{:T(128)S(6)} %add.131), dynamic_slice_sizes={1} | dynamic-slice | bytes 12
  11.1 1.2 %dynamic-slice = u32[1]{0:T(128)} dynamic-slice(u32[32]{0:T(128)} %constant.124, u32[]{:T(128)S(6)} %add.131), dynamic_slice_sizes={1} | dynamic-slice | bytes 12
  13.6 0.8 bitcast_dynamic-update-slice_fusion.1
  14.4 8.1 %all-reduce = s32[72]{0:T(128)S(1)} all-reduce(s32[72]{0:T(128)S(1)} %get-tuple-element.7), channel_id=2, replica_groups=mesh['col'=8,'row'=4] {'col'}, use_global_device_ids=true, to_apply=%add | all-reduce | flops 72 | bytes 576
  22.5 8.5 %all-reduce.1 = s32[36]{0:T(128)S(1)} all-reduce(s32[36]{0:T(128)S(1)} %get-tuple-element.8), channel_id=3, replica_groups=mesh['col'=8,'row'=4] {'row'}, use_global_device_ids=true, to_apply=%add.1 | all-reduce | flops 36 | bytes 288
  31.0 0.0 collective-permute-done
  31.0 0.0 collective-permute-start.2
  31.1 1.0 copy.29
  32.2 0.0 collective-permute-done.1
  32.2 2.7 %collective-permute-start.3 = (bf16[9,4096]{1,0:T(8,128)(2,1)S(1)}, bf16[9,4096]{1,0:T(8,128)(2,1)}, u32[]{:S(2)}, u32[]{:S(2)}) collective-permute-start(bf16[9,4096]{1,0:T(8,128)(2,1)S(1)} %collective-permute-done.1), channel_id=1, source_target_pairs={{0,28},{4,0},{8,4},{12,8},{16,12},{20,16},{24,20},{28,24},{1,29},{... | collective-permute-start | bytes 221192 | tf_op jit(solution)/shard_map/ppermute | solution.py:83
  34.9 1.8 %collective-permute-done.2 = bf16[9,4096]{1,0:T(8,128)(2,1)S(1)} collective-permute-done((bf16[9,4096]{1,0:T(8,128)(2,1)S(1)}, bf16[9,4096]{1,0:T(8,128)(2,1)S(1)}, u32[]{:S(2)}, u32[]{:S(2)}) %collective-permute-start.2) | collective-permute-done | bytes 73760 | tf_op jit(solution)/shard_map/ppermute | solution.py:78
  36.7 0.0 collective-permute-start.4
  36.7 16.2 %all-gather.2 = bf16[1,36,4096]{2,0,1:T(2,128)(2,1)S(1)} all-gather(bf16[1,9,4096]{2,0,1:T(2,128)(2,1)S(1)} %copy.29), channel_id=4, replica_groups=mesh['col'=8,'row'=4] {'row'}, dimensions={1}, use_global_device_ids=true | all-gather | bytes 368640 | tf_op jit(solution)/shard_map/all_gather | solution.py:44
  52.8 1.5 %scatter_custom_fusion = bf16[72,4096]{1,0:T(8,128)(2,1)S(1)} fusion(s32[36]{0:T(128)S(1)} %compare_select_fusion.2, bf16[1,36,4096]{2,0,1:T(2,128)(2,1)S(1)} %all-gather.2, bf16[]{:T(256)} %constant.102.clone.1), kind=kCustom, calls=%fused_computation.7 | custom fusion | bytes 1179650 | tf_op jit(solution)/shard_map/scatter | solution.py:53
  54.3 0.0 copy-start.1
  54.4 1.3 %reshape.74 = bf16[24,3,64,64]{3,2,1,0:T(8,128)(2,1)S(1)} reshape(bf16[72,4096]{1,0:T(8,128)(2,1)S(1)} %scatter_custom_fusion) | data formatting | bytes 1179648 | tf_op jit(solution)/shard_map/reshape | solution.py:54
  55.6 0.7 copy.30
  56.5 1.2 dynamic_update_slice.24
  57.6 0.0 collective-permute-done.3
  57.6 0.1 collective-permute-start.5
  57.7 0.5 collective-permute-start.6
  58.2 3.0 %gather_fusion = bf16[72,64,192]{1,2,0:T(8,128)(2,1)} fusion(bf16[24,64,192]{1,2,0:T(8,128)(2,1)S(1)} %bitcast.39, s32[1024]{0:T(1024)S(1)} %pad_clamp_fusion.1), kind=kCustom, calls=%fused_computation | custom fusion | bytes 3539232 | tf_op jit(solution)/shard_map/gather | solution.py:17
  61.2 0.7 dynamic_update_slice.25
  61.9 1.2 dynamic_update_slice.26
  63.1 1.0 dynamic_update_slice.27
  64.1 1.8 %dynamic_update_slice.28 = bf16[72,4096]{1,0:T(8,128)(2,1)S(1)} dynamic-update-slice(bf16[72,4096]{1,0:T(8,128)(2,1)S(1)} %dynamic_update_slice.27, bf16[9,4096]{1,0:T(8,128)(2,1)} %collective-permute-done.3, s32[]{:T(128)S(6)} %select_n.123, s32[]{:T(128)} %constant.100.clone.1) | dynamic-update-slice | bytes 147460 | tf_op jit(solution)/shard_map/dynamic_update_slice | solution.py:84
  65.9 1.8 %dynamic_update_slice.29 = bf16[72,4096]{1,0:T(8,128)(2,1)S(1)} dynamic-update-slice(bf16[72,4096]{1,0:T(8,128)(2,1)S(1)} %dynamic_update_slice.28, bf16[9,4096]{1,0:T(8,128)(2,1)} %collective-permute-done.4, s32[]{:T(128)S(6)} %select_n.125, s32[]{:T(128)} %constant.100.clone.1) | dynamic-update-slice | bytes 147460 | tf_op jit(solution)/shard_map/dynamic_update_slice | solution.py:79
  67.7 1.8 %dynamic_update_slice.30 = bf16[72,4096]{1,0:T(8,128)(2,1)S(1)} dynamic-update-slice(bf16[72,4096]{1,0:T(8,128)(2,1)S(1)} %dynamic_update_slice.29, bf16[9,4096]{1,0:T(8,128)(2,1)} %collective-permute-done.5, s32[]{:T(128)S(6)} %select_n.127, s32[]{:T(128)} %constant.100.clone.1) | dynamic-update-slice | bytes 147460 | tf_op jit(solution)/shard_map/dynamic_update_slice | solution.py:84
  69.5 0.0 collective-permute-done.6
  69.5 1.2 dynamic_update_slice.31
  70.7 1.3 %reshape.73 = bf16[72,64,64]{2,1,0:T(8,128)(2,1)S(1)} reshape(bf16[72,4096]{1,0:T(8,128)(2,1)S(1)} %dynamic_update_slice.31) | data formatting | bytes 1179648 | tf_op jit(solution)/shard_map/reshape | solution.py:18
  71.9 4.4 %fusion.19 = f32[72,64,192]{2,1,0:T(8,128)S(1)} fusion(bf16[72,64,64]{2,1,0:T(8,128)(2,1)S(1)} %reshape.73, bf16[72,64,192]{1,2,0:T(8,128)(2,1)} %gather_fusion), kind=kOutput, calls=%fused_computation.45 | convolution fusion | flops 113246208 | bytes 5898240 | tf_op jit(solution)/shard_map/mab,mbw->maw/dot_general | solution.py:19
  76.3 4.3 %fusion = f32[6,64,192]{2,0,1:T(8,128)S(1)} fusion(f32[72,64,192]{2,1,0:T(8,128)S(1)} %fusion.19, s32[72]{0:T(128)S(1)} %get-tuple-element.5), kind=kOutput, calls=%fused_computation.3 | convolution fusion | flops 63701424 | bytes 3834144 | tf_op jit(solution)/shard_map/mr,maw->raw/dot_general | solution.py:23
  80.6 0.1 copy.33
  80.7 0.9 copy.34
  81.6 0.0 all-gather.5.cloned.1.call-update
  81.6 1.3 %copy.36 = bf16[24,64,3,64]{1,0,3,2:T(8,128)(2,1)S(1)} copy(bf16[24,64,3,64]{3,1,2,0:T(8,128)(2,1)S(1)} %bitcast.38) | data formatting | bytes 1179648 | tf_op jit(solution)/shard_map/transpose | solution.py:55
  82.9 0.7 reshape_reshape.3
  83.7 26.5 %all-gather.5.cloned.1.call-done = f32[384,1536]{0,1:T(8,128)} async-done(((f32[384,192]{0,1:T(8,128)}), f32[384,1536]{0,1:T(8,128)}) %all-gather.5.cloned.1.call-update) | async-done | bytes 2359312 | tf_op jit(solution)/shard_map/all_gather | solution.py:97
  110.2 2.9 %fusion.2 = f32[384,192]{0,1:T(8,128)S(1)} fusion(f32[384,1536]{0,1:T(8,128)} %all-gather.5.cloned.1.call-done, bf16[1536,192]{0,1:T(8,128)(2,1)S(1)} %reshape_reshape.3, f32[384,192]{0,1:T(8,128)S(1)} %copy-done), kind=kOutput, calls=%fused_computation.6 | convolution fusion | flops 1359175680 | bytes 3538944 | tf_op jit(solution)/shard_map/dot_general | solution.py:96
  113.1 0.2 reshape.77
  113.3 0.3 copy.37
  113.6 0.2 reshape.78
  113.8 0.6 gather_fusion.1
  114.4 0.1 bitcast_select_fusion
  114.5 0.9 copy.38
  (17 shorter events, 0.1 us)
Async XLA Ops:
  6.5 103.6 %all-gather.5.cloned.1.call-start = ((), (), s32[]{:S(2)}) async-start(), calls=%async_computation | async-start | bytes 2654208 | tf_op jit(solution)/shard_map/all_gather | solution.py:97
  6.5 25.6 %collective-permute-start.1 = (bf16[9,4096]{1,0:T(8,128)(2,1)}, bf16[9,4096]{1,0:T(8,128)(2,1)S(1)}, u32[]{:S(2)}, u32[]{:S(2)}) collective-permute-start(bf16[9,4096]{1,0:T(8,128)(2,1)} %bitcast.42), channel_id=1, source_target_pairs={{0,28},{4,0},{8,4},{12,8},{16,12},{20,16},{24,20},{28,24},{1,29},{... | collective-permute-start | bytes 221192 | tf_op jit(solution)/shard_map/ppermute | solution.py:83
  9.9 21.1 %collective-permute-start = (bf16[9,4096]{1,0:T(8,128)(2,1)}, bf16[9,4096]{1,0:T(8,128)(2,1)S(1)}, u32[]{:S(2)}, u32[]{:S(2)}) collective-permute-start(bf16[9,4096]{1,0:T(8,128)(2,1)} %bitcast.43), channel_id=1, source_target_pairs={{0,4},{4,8},{8,12},{12,16},{16,20},{20,24},{24,28},{28,0},{1,5},{5... | collective-permute-start | bytes 221192 | tf_op jit(solution)/shard_map/ppermute | solution.py:78
  31.0 5.7 %collective-permute-start.2 = (bf16[9,4096]{1,0:T(8,128)(2,1)S(1)}, bf16[9,4096]{1,0:T(8,128)(2,1)S(1)}, u32[]{:S(2)}, u32[]{:S(2)}) collective-permute-start(bf16[9,4096]{1,0:T(8,128)(2,1)S(1)} %collective-permute-done), channel_id=1, source_target_pairs={{0,4},{4,8},{8,12},{12,16},{16,20},{20,24},{24,28},{28,0},{1,5},{5... | collective-permute-start | bytes 221192 | tf_op jit(solution)/shard_map/ppermute | solution.py:78
  32.2 25.4 %collective-permute-start.3 = (bf16[9,4096]{1,0:T(8,128)(2,1)S(1)}, bf16[9,4096]{1,0:T(8,128)(2,1)}, u32[]{:S(2)}, u32[]{:S(2)}) collective-permute-start(bf16[9,4096]{1,0:T(8,128)(2,1)S(1)} %collective-permute-done.1), channel_id=1, source_target_pairs={{0,28},{4,0},{8,4},{12,8},{16,12},{20,16},{24,20},{28,24},{1,29},{... | collective-permute-start | bytes 221192 | tf_op jit(solution)/shard_map/ppermute | solution.py:83
  36.7 21.0 %collective-permute-start.4 = (bf16[9,4096]{1,0:T(8,128)(2,1)S(1)}, bf16[9,4096]{1,0:T(8,128)(2,1)}, u32[]{:S(2)}, u32[]{:S(2)}) collective-permute-start(bf16[9,4096]{1,0:T(8,128)(2,1)S(1)} %collective-permute-done.2), channel_id=1, source_target_pairs={{0,4},{4,8},{8,12},{12,16},{16,20},{20,24},{24,28},{28,0},{1,5},{5... | collective-permute-start | bytes 221192 | tf_op jit(solution)/shard_map/ppermute | solution.py:78
  54.3 2.1 %copy-start.1 = (bf16[1,9,4096]{2,1,0:T(8,128)(2,1)S(1)}, bf16[1,9,4096]{2,1,0:T(8,128)(2,1)}, u32[]{:S(2)}) copy-start(bf16[1,9,4096]{2,1,0:T(8,128)(2,1)} %param.3) | copy-start | bytes 221188
  57.6 10.0 %collective-permute-start.5 = (bf16[9,4096]{1,0:T(8,128)(2,1)}, bf16[9,4096]{1,0:T(8,128)(2,1)}, u32[]{:S(2)}, u32[]{:S(2)}) collective-permute-start(bf16[9,4096]{1,0:T(8,128)(2,1)} %collective-permute-done.3), channel_id=1, source_target_pairs={{0,28},{4,0},{8,4},{12,8},{16,12},{20,16},{24,20},{28,24},{1,29},{... | collective-permute-start | bytes 221192 | tf_op jit(solution)/shard_map/ppermute | solution.py:83
  57.7 11.8 %collective-permute-start.6 = (bf16[9,4096]{1,0:T(8,128)(2,1)}, bf16[9,4096]{1,0:T(8,128)(2,1)S(1)}, u32[]{:S(2)}, u32[]{:S(2)}) collective-permute-start(bf16[9,4096]{1,0:T(8,128)(2,1)} %collective-permute-done.4), channel_id=1, source_target_pairs={{0,4},{4,8},{8,12},{12,16},{16,20},{20,24},{24,28},{28,0},{1,5},{5... | collective-permute-start | bytes 221192 | tf_op jit(solution)/shard_map/ppermute | solution.py:78
  81.6 2.1 %copy-start.2 = (s32[1,13]{1,0:T(1,128)S(1)}, s32[1,13]{1,0:T(1,128)}, u32[]{:S(2)}) copy-start(s32[1,13]{1,0:T(1,128)} %param.5) | copy-start | bytes 160
  81.6 28.6 %copy-start = (f32[384,192]{0,1:T(8,128)S(1)}, f32[384,192]{0,1:T(8,128)}, u32[]{:S(2)}) copy-start(f32[384,192]{0,1:T(8,128)} %copy.34) | copy-start | bytes 884740
Sparse Core Ops, SparseCore 0:
  81.7 28.3 all-gather.4
